TPU v7x, 256 devices: a whole 4x4x8 slice. The times are simulated.
256 devices in a mesh: sens: 64 (over x, z_hi, y), grp: 4 (over z_lo, core).
Axes of the slice: x: 4, y: 4, z: 8 (z_hi: 4, z_lo: 2; z = z_hi * 2 + z_lo), core: 2. Of those that a mesh axis runs over, the one named last changes fastest.
Arguments:
- histories: bfloat16 [2048, 4096], P('sens', 'grp'), may hold values from -6 to 6
- bin_index: int32 [16], replicated, may hold values from 1 to 2047
- delays: int32 [2048, 4096], P('sens'), may hold values from 0 to 4095
- map_adjoint: float32 [4096], replicated, may hold values from -48 to 48
Outputs:
- history_adjoint: bfloat16 [2048, 4096], P('sens', 'grp')
Inputs may be any that keep to these rules, and one draw needn't show every extreme that they name: `delays`: each delay is already reduced modulo 4096.
All inputs are finite; a program needn't handle non-finite values.
Results may differ from a plain program's by a relative error of at most 0.0059.
Values may be sent and summed in bfloat16 or wider, within the bound.
No kernel may reach another device: no remote copies, remote signals or barrier semaphores. Data moves between devices by JAX's collectives and lax.ppermute only.
A program may use at most 64 MiB of HBM per device.

v0:
```python
import math
import jax
import jax.numpy as jnp
from jax import lax
from jax.sharding import PartitionSpec as P

NT = 4096
two_pi = 2.0 * math.pi


def transform_rows(first, count, bin_index, length):
    sample_times = first + lax.iota(jnp.int32, count)
    phase_index = sample_times[:, None] * bin_index[None, :] % length
    phase_angle = phase_index.astype(jnp.float32) * (two_pi / length)
    factor = 1.0 / math.sqrt(length)
    cosine = jnp.cos(phase_angle) * factor
    sine_part = -jnp.sin(phase_angle) * factor
    return jnp.concatenate([cosine, sine_part], 1).astype(jnp.bfloat16)


def circle_point(phase_index, length):
    eighth_bits = (length // 8).bit_length() - 1
    quarter = length // 4
    quadrant = phase_index >> eighth_bits + 1
    rest = phase_index & quarter - 1
    flip = rest >> eighth_bits & (rest != length // 8).astype(jnp.int32)
    folded = jnp.where(flip == 1, quarter - rest, rest)
    x = folded.astype(jnp.float32) * (two_pi / length)
    x2 = x * x
    sin_x = x * (1.0 + x2 * (-1.0 / 6.0 + x2 * (1.0 / 120.0 + x2 * (-1.0 / 5040.0))))
    cos_x = 1.0 + x2 * (-0.5 + x2 * (1.0 / 24.0 + x2 * (-1.0 / 720.0 + x2 * (1.0 / 40320.0))))
    swap = quadrant & 1 ^ flip == 1
    sine = jnp.where(swap, cos_x, sin_x)
    cosine = jnp.where(swap, sin_x, cos_x)
    sine = jnp.where(quadrant >= 2, -sine, sine)
    cosine = jnp.where((quadrant ^ quadrant >> 1) & 1 == 1, -cosine, cosine)
    return (cosine, sine)


def shifted(x, axis, shift):
    count = lax.axis_size(axis)
    return lax.ppermute(x, axis, [(j, (j + shift) % count) for j in range(count)])


def gather_stack(x, axis):
    count = lax.axis_size(axis)
    me = lax.axis_index(axis)
    stack = jnp.stack([x] + [shifted(x, axis, shift) for shift in range(1, count)])
    return stack[(me - jnp.arange(count)) % count]


def scatter_sum(x, axis):
    count = lax.axis_size(axis)
    lead = x.shape[:-1]
    parts = x.reshape(lead + (count, x.shape[-1] // count))
    parts = jnp.moveaxis(parts, -2, 0).reshape(count, -1)
    total = jnp.sum(lax.all_to_all(parts, axis, 0, 0, tiled=True), axis=0)
    return total.reshape(lead + (x.shape[-1] // count,))


def gather_last(x, axis):
    count = lax.axis_size(axis)
    copies = jnp.broadcast_to(x.reshape(1, -1), (count, x.size))
    joined = lax.all_to_all(copies, axis, 0, 0, tiled=True).reshape((count,) + x.shape)
    joined = jnp.moveaxis(joined, 0, -2)
    return joined.reshape(x.shape[:-1] + (count * x.shape[-1],))


def on_device(histories, bin_index, delays, map_adjoint):
    groups = lax.axis_size("grp")
    position = lax.axis_index("grp")
    bins = bin_index.shape[0]
    sensors = delays.shape[0] * lax.axis_size(SENS_AXES)
    steer_scale = 1.0 / math.sqrt(sensors)
    samples = histories.shape[1]
    scan_share = delays.shape[1] // groups
    transform = transform_rows(position * samples, samples, bin_index, NT)
    spectra = jnp.dot(histories, transform, preferred_element_type=jnp.float32)
    spectra = jnp.sum(gather_stack(spectra, "grp"), axis=0)
    real_t = spectra[:, :bins].T
    imag_t = spectra[:, bins:].T
    own_delays = lax.dynamic_slice_in_dim(delays, position * scan_share, scan_share, 1)
    own_weight = 2.0 * lax.dynamic_slice_in_dim(map_adjoint, position * scan_share, scan_share, 0)
    phase_index = bin_index[:, None, None] * own_delays[None, :, :] & NT - 1
    cosine, sine_part = lax.optimization_barrier(circle_point(phase_index, NT))
    steer_real = jnp.sum(real_t[:, :, None] * cosine - imag_t[:, :, None] * sine_part, axis=1)
    steer_imag = jnp.sum(real_t[:, :, None] * sine_part + imag_t[:, :, None] * cosine, axis=1)
    steered = jnp.stack([steer_real, steer_imag]) * steer_scale
    offset = 0
    for axis in SENS_AXES:
        offset = offset * lax.axis_size(axis) + lax.axis_index(axis)
    count = lax.axis_size(SENS_AXES)
    parts = steered.reshape(count, steered.size // count)
    width = parts.shape[1]
    chunk = jnp.sum(lax.all_to_all(parts, SENS_AXES, 0, 0, tiled=True), axis=0)
    start = offset * width % scan_share
    chunk = lax.dynamic_slice_in_dim(own_weight, start, width, 0) * chunk
    bar = lax.all_gather(chunk, SENS_AXES, tiled=True).reshape(steered.shape)
    bar_real = bar[0]
    bar_imag = bar[1]
    back_real = jnp.sum(bar_real[:, None, :] * cosine + bar_imag[:, None, :] * sine_part, axis=2)
    back_imag = jnp.sum(bar_imag[:, None, :] * cosine - bar_real[:, None, :] * sine_part, axis=2)
    back = jnp.concatenate([back_real.T, back_imag.T], 1) * steer_scale
    back = jnp.sum(gather_stack(back, "grp"), axis=0)
    adjoint = back.astype(jnp.bfloat16)
    local_part = lax.dot_general(
        adjoint, transform, (((1,), (1,)), ((), ())), preferred_element_type=jnp.float32
    )
    return local_part.astype(jnp.bfloat16)


SENS_AXES = ("sx", "sz", "sy")


def solution(mesh):
    sens_size = mesh.shape["sens"]
    side = round(sens_size ** (1.0 / 3.0))
    assert side**3 == sens_size
    fine = jax.sharding.Mesh(
        mesh.devices.reshape(side, side, side, mesh.shape["grp"]), SENS_AXES + ("grp",)
    )
    placed = (P(SENS_AXES, "grp"), P(), P(SENS_AXES, None), P())
    return jax.shard_map(
        on_device, mesh=fine, in_specs=placed, out_specs=P(SENS_AXES, "grp"), check_vma=False
    )
```

profile of v0, /device:TPU:1, one launch (start us, length us, event | category | flops | bytes accessed | tf_op | source)
XLA Modules:
  0.0 237.5 jit_solution(9495438284824854974)
XLA Ops:
  0.0 0.0 copy-start
  0.0 1.1 multiply_convert_fusion.1
  1.1 1.0 fusion.13
  2.0 3.0 %collective-permute-start = (f32[32,32]{0,1:T(8,128)S(1)}, f32[32,32]{0,1:T(8,128)S(1)}, u32[]{:S(2)}, u32[]{:S(2)}) collective-permute-start(f32[32,32]{0,1:T(8,128)S(1)} %bitcast.32), channel_id=1, source_target_pairs={{0,1},{1,2},{2,3},{3,0},{4,5},{5,6},{6,7},{7,4},{8,9},{9,10},{10,1... | collective-permute-start | bytes 12296 | tf_op jit(solution)/shard_map/ppermute | solution.py:42
  5.1 1.5 collective-permute-start.1
  6.6 0.0 collective-permute-start.2
  6.6 0.0 copy-done
  6.7 4.8 %negate_select_fusion = (f32[16,32,1024]{2,1,0:T(8,128)S(1)}, f32[16,32,1024]{2,1,0:T(8,128)}) fusion(s32[32,1024]{1,0:T(8,128)S(1)} %constant_dynamic-slice_fusion, s32[16]{0:T(128)} %param.5), kind=kLoop, calls=%fused_computation.2 | loop fusion | flops 22544384 | bytes 4325440 | tf_op jit(solution)/shard_map/jit(_where)/select_n | solution.py:35
  11.4 0.0 collective-permute-done
  11.4 0.0 collective-permute-done.1
  11.5 0.0 collective-permute-done.2
  11.5 0.6 gather_fusion
  12.1 3.1 %subtract_reduce_fusion.1 = (f32[16,1024]{1,0:T(8,128)S(1)}, f32[16,1024]{1,0:T(8,128)S(1)}) fusion(f32[16,32,1024]{2,1,0:T(8,128)S(1)} %get-tuple-element.8, f32[16,32,1024]{2,1,0:T(8,128)} %get-tuple-element.7, f32[16,32]{1,0:T(8,128)S(1)} %get-tuple-element.18, f32[16,32]{1,0:T(8,128)S(1)} %get-tuple-element.17), kind=kLoop, calls=%fused_computation.13 | loop fusion | flops 4161536 | bytes 4329472 | tf_op jit(solution)/shard_map/reduce_sum | solution.py:86
  15.2 0.8 mul.239
  16.0 12.6 %all-to-all-start = ((f32[64,1,512]{2,1,0:T(1,128)}), f32[64,1,512]{2,1,0:T(1,128)S(1)}, u32[]{:S(2)}, u32[]{:S(2)}) async-start(f32[64,1,512]{2,1,0:T(1,128)} %mul.239), calls=%async_computation | async-start | bytes 262144 | tf_op jit(solution)/shard_map/all_to_all | solution.py:95
  28.6 0.7 dynamic-slice_multiply_fusion
  29.3 10.7 %all-to-all-done = f32[64,1,512]{2,1,0:T(1,128)S(1)} async-done(((f32[64,1,512]{2,1,0:T(1,128)}), f32[64,1,512]{2,1,0:T(1,128)S(1)}, u32[]{:S(2)}, u32[]{:S(2)}) %all-to-all-start) | async-done | bytes 131104 | tf_op jit(solution)/shard_map/all_to_all | solution.py:95
  40.0 0.1 reduce_sum.66
  40.1 0.1 dynamic-slice_multiply_fusion.1
  40.2 157.9 %all-gather = f32[64,1,512]{2,1,0:T(1,128)S(1)} all-gather(f32[1,1,512]{2,1,0:T(1,128)S(1)} %bitcast.42), channel_id=1, replica_groups=mesh['sx'=4,'sz'=4,'sy'=4,'grp'=4] {'sx','sz','sy'}, dimensions={0}, use_global_device_ids=true | all-gather | bytes 133120 | tf_op jit(solution)/shard_map/all_gather | solution.py:98
  198.1 0.3 slice_reduce_fusion.1
  198.5 2.3 add_reduce_fusion
  200.8 31.0 %collective-permute-start.3 = (f32[32,32]{0,1:T(8,128)S(1)}, f32[32,32]{0,1:T(8,128)S(1)}, u32[]{:S(2)}, u32[]{:S(2)}) collective-permute-start(f32[32,32]{0,1:T(8,128)S(1)} %maximum_multiply_fusion.2), channel_id=1, source_target_pairs={{0,1},{1,2},{2,3},{3,0},{4,5},{5,6},{6,7},{7,4},{8,9},{9,10},{10,1... | collective-permute-start | bytes 12296 | tf_op jit(solution)/shard_map/ppermute | solution.py:42
  231.9 1.1 collective-permute-start.4
  232.9 0.0 collective-permute-start.5
  232.9 0.0 collective-permute-done.3
  232.9 1.5 collective-permute-done.4
  234.4 1.6 collective-permute-done.5
  236.1 0.6 gather_fusion.1
  236.7 0.8 convolution_convert_fusion
  (14 shorter events, 0.2 us)
Async XLA Ops:
  0.0 6.6 %copy-start = (s32[32,4096]{1,0:T(8,128)S(1)}, s32[32,4096]{1,0:T(8,128)}, u32[]{:S(2)}) copy-start(s32[32,4096]{1,0:T(8,128)} %param.6) | copy-start | bytes 1572868
  2.0 9.4 %collective-permute-start = (f32[32,32]{0,1:T(8,128)S(1)}, f32[32,32]{0,1:T(8,128)S(1)}, u32[]{:S(2)}, u32[]{:S(2)}) collective-permute-start(f32[32,32]{0,1:T(8,128)S(1)} %bitcast.32), channel_id=1, source_target_pairs={{0,1},{1,2},{2,3},{3,0},{4,5},{5,6},{6,7},{7,4},{8,9},{9,10},{10,1... | collective-permute-start | bytes 12296 | tf_op jit(solution)/shard_map/ppermute | solution.py:42
  5.1 6.4 %collective-permute-start.1 = (f32[32,32]{0,1:T(8,128)S(1)}, f32[32,32]{0,1:T(8,128)S(1)}, u32[]{:S(2)}, u32[]{:S(2)}) collective-permute-start(f32[32,32]{0,1:T(8,128)S(1)} %bitcast.33), channel_id=1, source_target_pairs={{0,2},{1,3},{2,0},{3,1},{4,6},{5,7},{6,4},{7,5},{8,10},{9,11},{10,... | collective-permute-start | bytes 12296 | tf_op jit(solution)/shard_map/ppermute | solution.py:42
  6.6 4.8 %collective-permute-start.2 = (f32[32,32]{0,1:T(8,128)S(1)}, f32[32,32]{0,1:T(8,128)S(1)}, u32[]{:S(2)}, u32[]{:S(2)}) collective-permute-start(f32[32,32]{0,1:T(8,128)S(1)} %bitcast.34), channel_id=1, source_target_pairs={{0,3},{1,0},{2,1},{3,2},{4,7},{5,4},{6,5},{7,6},{8,11},{9,8},{10,9... | collective-permute-start | bytes 12296 | tf_op jit(solution)/shard_map/ppermute | solution.py:42
  16.0 24.0 %all-to-all-start = ((f32[64,1,512]{2,1,0:T(1,128)}), f32[64,1,512]{2,1,0:T(1,128)S(1)}, u32[]{:S(2)}, u32[]{:S(2)}) async-start(f32[64,1,512]{2,1,0:T(1,128)} %mul.239), calls=%async_computation | async-start | bytes 262144 | tf_op jit(solution)/shard_map/all_to_all | solution.py:95
  200.8 32.1 %collective-permute-start.3 = (f32[32,32]{0,1:T(8,128)S(1)}, f32[32,32]{0,1:T(8,128)S(1)}, u32[]{:S(2)}, u32[]{:S(2)}) collective-permute-start(f32[32,32]{0,1:T(8,128)S(1)} %maximum_multiply_fusion.2), channel_id=1, source_target_pairs={{0,1},{1,2},{2,3},{3,0},{4,5},{5,6},{6,7},{7,4},{8,9},{9,10},{10,1... | collective-permute-start | bytes 12296 | tf_op jit(solution)/shard_map/ppermute | solution.py:42
  231.9 2.6 %collective-permute-start.4 = (f32[32,32]{0,1:T(8,128)S(1)}, f32[32,32]{0,1:T(8,128)S(1)}, u32[]{:S(2)}, u32[]{:S(2)}) collective-permute-start(f32[32,32]{0,1:T(8,128)S(1)} %maximum_multiply_fusion.2), channel_id=1, source_target_pairs={{0,2},{1,3},{2,0},{3,1},{4,6},{5,7},{6,4},{7,5},{8,10},{9,11},{10,... | collective-permute-start | bytes 12296 | tf_op jit(solution)/shard_map/ppermute | solution.py:42
  232.9 3.2 %collective-permute-start.5 = (f32[32,32]{0,1:T(8,128)S(1)}, f32[32,32]{0,1:T(8,128)S(1)}, u32[]{:S(2)}, u32[]{:S(2)}) collective-permute-start(f32[32,32]{0,1:T(8,128)S(1)} %maximum_multiply_fusion.2), channel_id=1, source_target_pairs={{0,3},{1,0},{2,1},{3,2},{4,7},{5,4},{6,5},{7,6},{8,11},{9,8},{10,9... | collective-permute-start | bytes 12296 | tf_op jit(solution)/shard_map/ppermute | solution.py:42
where the time goes:
time: 238 us
  blocking collectives  158 us (66%)
  starting transfers between devices  49.2 us (21%)
  waiting for transfers between devices  13.9 us (6%)
  other arithmetic  12.2 us (5%)
    all_gather x1, blocking collectives, on_device(): bar = lax.all_gather(chunk, SENS_AXES, tiled=True).reshape(steered.shape)  158 us
    ppermute x6, starting transfers between devices, shifted(): lax.ppermute(x, axis, [(j, (j + shift) % count) for j in range(count)])  36.7 us
    all_to_all x1, starting transfers between devices, on_device(): chunk = jnp.sum(lax.all_to_all(parts, SENS_AXES, 0, 0, tiled=True), axis=0)  12.6 us
    all_to_all x1, waiting for transfers between devices, on_device(): chunk = jnp.sum(lax.all_to_all(parts, SENS_AXES, 0, 0, tiled=True), axis=0)  10.7 us
    select_n x1, other arithmetic, circle_point(): sine = jnp.where(quadrant >= 2, -sine, sine)  4.77 us
  transfers between devices with their start and end apart: 7, of which 3 were waited for; matrix products, arithmetic and copies ran while one was open for 2% of the time, Pallas kernels for 0%

commit v1 on v0

--- a/solution.py
+++ b/solution.py
@@ -95,7 +95,9 @@
     chunk = jnp.sum(lax.all_to_all(parts, SENS_AXES, 0, 0, tiled=True), axis=0)
     start = offset * width % scan_share
     chunk = lax.dynamic_slice_in_dim(own_weight, start, width, 0) * chunk
-    bar = lax.all_gather(chunk, SENS_AXES, tiled=True).reshape(steered.shape)
+    bar = jnp.concatenate(
+        lax.all_to_all(jnp.stack([chunk] * lax.axis_size(SENS_AXES)), SENS_AXES, 0, 0), axis=0
+    ).reshape(steered.shape)
     bar_real = bar[0]
     bar_imag = bar[1]
     back_real = jnp.sum(bar_real[:, None, :] * cosine + bar_imag[:, None, :] * sine_part, axis=2)

time: 238 us -> 68.8 us (0.29)
  blocking collectives: 158 us -> 15.7 us
  starting transfers between devices: 49.2 us -> 22.3 us
    all_gather x1 -> x0, blocking collectives: 158 us -> none  [on_device(): bar = lax.all_gather(chunk, SENS_AXES, tiled=True).reshape(steered.shape)]
    ppermute x6, starting transfers between devices: 36.7 us -> 9.76 us  [shifted(): lax.ppermute(x, axis, [(j, (j + shift) % count) for j in range(count)])]
    all_to_all x0 -> x1, blocking collectives: none -> 15.7 us  [on_device(): lax.all_to_all(jnp.stack([chunk] * lax.axis_size(SENS_AXES)), SENS_AXES,...]
  transfers between devices with their start and end apart: 7 -> 7, of which waited for: 3 -> 4; matrix products, arithmetic and copies ran while one was open for 2% -> 8% of each run, Pallas kernels for 0% -> 0%
where the time goes in v1:
time: 68.8 us; the launch traced here: 68.4 us
  starting transfers between devices  22.3 us (32%)
  blocking collectives  15.7 us (23%)
  waiting for transfers between devices  13.9 us (20%)
  other arithmetic  12.2 us (18%)
  local copies, waits for them, and re-layouts  2.38 us (3%)
  matrix products  1.79 us (3%)
    all_to_all x1, blocking collectives, on_device(): lax.all_to_all(jnp.stack([chunk] * lax.axis_size(SENS_AXES)), SENS_AXES,...  15.7 us
    all_to_all x1, starting transfers between devices, on_device(): chunk = jnp.sum(lax.all_to_all(parts, SENS_AXES, 0, 0, tiled=True), axis=0)  12.6 us
    all_to_all x1, waiting for transfers between devices, on_device(): chunk = jnp.sum(lax.all_to_all(parts, SENS_AXES, 0, 0, tiled=True), axis=0)  10.7 us
    ppermute x6, starting transfers between devices, shifted(): lax.ppermute(x, axis, [(j, (j + shift) % count) for j in range(count)])  9.76 us
    select_n x1, other arithmetic, circle_point(): sine = jnp.where(quadrant >= 2, -sine, sine)  4.77 us
    ppermute x6, waiting for transfers between devices, shifted(): lax.ppermute(x, axis, [(j, (j + shift) % count) for j in range(count)])  3.16 us
    reduce_sum x1, other arithmetic, on_device(): jnp.sum(real_t[:, :, None] * cosine - imag_t[:, :, None] * sine_part, axi...  3.09 us
    reduce_sum x1, other arithmetic, on_device(): jnp.sum(bar_real[:, None, :] * cosine + bar_imag[:, None, :] * sine_part,...  2.32 us
  transfers between devices with their start and end apart: 7, of which 4 were waited for; matrix products, arithmetic and copies ran while one was open for 8% of the time, Pallas kernels for 0%

profile of v1, /device:TPU:1, one launch (start us, length us, event | category | flops | bytes accessed | tf_op | source)
XLA Modules:
  0.0 68.4 jit_solution(2975510089621858343)
XLA Ops:
  0.0 0.0 copy-start
  0.0 1.1 %multiply_convert_fusion.1 = (bf16[1024,16]{0,1:T(8,128)(2,1)S(1)}, bf16[1024,16]{0,1:T(8,128)(2,1)S(1)}) fusion(s32[16]{0:T(128)} %param.5, s32[1024]{0:T(1024)S(1)} %iota_add_fusion), kind=kLoop, calls=%fused_computation.42 | loop fusion | flops 311296 | bytes 69696 | tf_op jit(solution)/shard_map/convert
  1.1 1.0 %fusion.13 = f32[32,32]{1,0:T(8,128)S(1)} fusion(bf16[32,1024]{1,0:T(8,128)(2,1)} %param.4, bf16[1024,16]{0,1:T(8,128)(2,1)S(1)} %get-tuple-element.20, bf16[1024,16]{0,1:T(8,128)(2,1)S(1)} %get-tuple-element.19), kind=kOutput, calls=%fused_computation.43 | convolution fusion | flops 2228224 | bytes 135168 | tf_op jit(solution)/shard_map/dot_general | solution.py:78
  2.0 3.0 %collective-permute-start = (f32[32,32]{0,1:T(8,128)S(1)}, f32[32,32]{0,1:T(8,128)S(1)}, u32[]{:S(2)}, u32[]{:S(2)}) collective-permute-start(f32[32,32]{0,1:T(8,128)S(1)} %bitcast.31), channel_id=1, source_target_pairs={{0,1},{1,2},{2,3},{3,0},{4,5},{5,6},{6,7},{7,4},{8,9},{9,10},{10,1... | collective-permute-start | bytes 12296 | tf_op jit(solution)/shard_map/ppermute | solution.py:42
  5.1 1.5 %collective-permute-start.1 = (f32[32,32]{0,1:T(8,128)S(1)}, f32[32,32]{0,1:T(8,128)S(1)}, u32[]{:S(2)}, u32[]{:S(2)}) collective-permute-start(f32[32,32]{0,1:T(8,128)S(1)} %bitcast.32), channel_id=1, source_target_pairs={{0,2},{1,3},{2,0},{3,1},{4,6},{5,7},{6,4},{7,5},{8,10},{9,11},{10,... | collective-permute-start | bytes 12296 | tf_op jit(solution)/shard_map/ppermute | solution.py:42
  6.6 0.0 collective-permute-start.2
  6.6 0.0 copy-done
  6.7 4.8 %negate_select_fusion = (f32[16,32,1024]{2,1,0:T(8,128)S(1)}, f32[16,32,1024]{2,1,0:T(8,128)}) fusion(s32[32,1024]{1,0:T(8,128)S(1)} %constant_dynamic-slice_fusion, s32[16]{0:T(128)} %param.5), kind=kLoop, calls=%fused_computation.2 | loop fusion | flops 22544384 | bytes 4325440 | tf_op jit(solution)/shard_map/jit(_where)/select_n | solution.py:35
  11.4 0.0 collective-permute-done
  11.4 0.0 collective-permute-done.1
  11.5 0.0 collective-permute-done.2
  11.5 0.6 gather_fusion
  12.1 3.1 %subtract_reduce_fusion.1 = (f32[16,1024]{1,0:T(8,128)S(1)}, f32[16,1024]{1,0:T(8,128)S(1)}) fusion(f32[16,32,1024]{2,1,0:T(8,128)S(1)} %get-tuple-element.8, f32[16,32,1024]{2,1,0:T(8,128)} %get-tuple-element.7, f32[16,32]{1,0:T(8,128)S(1)} %get-tuple-element.18, f32[16,32]{1,0:T(8,128)S(1)} %get-tuple-element.17), kind=kLoop, calls=%fused_computation.13 | loop fusion | flops 4161536 | bytes 4329472 | tf_op jit(solution)/shard_map/reduce_sum | solution.py:86
  15.2 0.8 %mul.245 = f32[64,1,512]{2,1,0:T(1,128)} reshape(f32[2,16,1024]{2,1,0:T(8,128)S(1)} %maximum_multiply_fusion) | data formatting | bytes 262144 | tf_op jit(solution)/shard_map/mul | solution.py:88
  16.0 12.6 %all-to-all-start = ((f32[64,1,512]{2,1,0:T(1,128)}), f32[64,1,512]{2,1,0:T(1,128)S(1)}, u32[]{:S(2)}, u32[]{:S(2)}) async-start(f32[64,1,512]{2,1,0:T(1,128)} %mul.245), calls=%async_computation | async-start | bytes 262144 | tf_op jit(solution)/shard_map/all_to_all | solution.py:95
  28.6 0.7 %dynamic-slice_multiply_fusion = f32[1024]{0:T(1024)S(1)} fusion(f32[4096]{0:T(1024)} %param.7, s32[]{:T(128)S(6)} %select_n.63), kind=kLoop, calls=%fused_computation.51 | loop fusion | flops 1024 | bytes 8196 | tf_op jit(solution)/shard_map/mul | solution.py:83
  29.3 10.7 %all-to-all-done = f32[64,1,512]{2,1,0:T(1,128)S(1)} async-done(((f32[64,1,512]{2,1,0:T(1,128)}), f32[64,1,512]{2,1,0:T(1,128)S(1)}, u32[]{:S(2)}, u32[]{:S(2)}) %all-to-all-start) | async-done | bytes 131104 | tf_op jit(solution)/shard_map/all_to_all | solution.py:95
  40.0 0.1 reduce_sum.66
  40.1 0.1 dynamic-slice_multiply_fusion.1
  40.2 0.1 stack.34
  40.3 15.7 %all_to_all.12 = f32[64,1,512]{2,1,0:T(1,128)S(1)} all-to-all(f32[64,1,512]{2,1,0:T(1,128)S(1)} %stack.34), channel_id=1, replica_groups=mesh['sx'=4,'sz'=4,'sy'=4,'grp'=4] {'sx','sz','sy'}, dimensions={0} | all-to-all | bytes 262144 | tf_op jit(solution)/shard_map/all_to_all | solution.py:99
  55.9 0.3 slice_reduce_fusion.1
  56.3 2.3 %add_reduce_fusion = (f32[16,32]{1,0:T(8,128)S(1)}, f32[16,32]{1,0:T(8,128)S(1)}) fusion(f32[16,32,1024]{2,1,0:T(8,128)S(1)} %get-tuple-element.8, f32[16,32,1024]{2,1,0:T(8,128)} %get-tuple-element.7, f32[16,1024]{1,0:T(8,128)S(1)} %mul.236, f32[16,1024]{1,0:T(8,128)S(1)} %mul.233), kind=kLoop, calls=%fused_computation.11 | loop fusion | flops 4193280 | bytes 4329472 | tf_op jit(solution)/shard_map/reduce_sum | solution.py:103
  58.7 4.4 %collective-permute-start.3 = (f32[32,32]{0,1:T(8,128)S(1)}, f32[32,32]{0,1:T(8,128)S(1)}, u32[]{:S(2)}, u32[]{:S(2)}) collective-permute-start(f32[32,32]{0,1:T(8,128)S(1)} %maximum_multiply_fusion.2), channel_id=1, source_target_pairs={{0,1},{1,2},{2,3},{3,0},{4,5},{5,6},{6,7},{7,4},{8,9},{9,10},{10,1... | collective-permute-start | bytes 12296 | tf_op jit(solution)/shard_map/ppermute | solution.py:42
  63.1 0.8 %collective-permute-start.4 = (f32[32,32]{0,1:T(8,128)S(1)}, f32[32,32]{0,1:T(8,128)S(1)}, u32[]{:S(2)}, u32[]{:S(2)}) collective-permute-start(f32[32,32]{0,1:T(8,128)S(1)} %maximum_multiply_fusion.2), channel_id=1, source_target_pairs={{0,2},{1,3},{2,0},{3,1},{4,6},{5,7},{6,4},{7,5},{8,10},{9,11},{10,... | collective-permute-start | bytes 12296 | tf_op jit(solution)/shard_map/ppermute | solution.py:42
  63.9 0.0 collective-permute-start.5
  63.9 0.1 collective-permute-done.3
  63.9 2.2 %collective-permute-done.4 = f32[32,32]{0,1:T(8,128)S(1)} collective-permute-done((f32[32,32]{0,1:T(8,128)S(1)}, f32[32,32]{0,1:T(8,128)S(1)}, u32[]{:S(2)}, u32[]{:S(2)}) %collective-permute-start.4) | collective-permute-done | bytes 4128 | tf_op jit(solution)/shard_map/ppermute | solution.py:42
  66.1 0.9 %collective-permute-done.5 = f32[32,32]{0,1:T(8,128)S(1)} collective-permute-done((f32[32,32]{0,1:T(8,128)S(1)}, f32[32,32]{0,1:T(8,128)S(1)}, u32[]{:S(2)}, u32[]{:S(2)}) %collective-permute-start.5) | collective-permute-done | bytes 4128 | tf_op jit(solution)/shard_map/ppermute | solution.py:42
  67.0 0.6 gather_fusion.1
  67.6 0.8 %convolution_convert_fusion = bf16[32,1024]{1,0:T(8,128)(2,1)} fusion(bf16[1024,16]{0,1:T(8,128)(2,1)S(1)} %get-tuple-element.20, bf16[1024,16]{0,1:T(8,128)(2,1)S(1)} %get-tuple-element.19, bf16[32,32]{0,1:T(8,128)(2,1)S(1)} %reduce_sum.69), kind=kOutput, calls=%fused_computation.26 | convolution fusion | flops 2260992 | bytes 133120 | tf_op jit(solution)/shard_map/dot_general | solution.py:108
  (14 shorter events, 0.2 us)
Async XLA Ops:
  0.0 6.6 %copy-start = (s32[32,4096]{1,0:T(8,128)S(1)}, s32[32,4096]{1,0:T(8,128)}, u32[]{:S(2)}) copy-start(s32[32,4096]{1,0:T(8,128)} %param.6) | copy-start | bytes 1572868
  2.0 9.4 %collective-permute-start = (f32[32,32]{0,1:T(8,128)S(1)}, f32[32,32]{0,1:T(8,128)S(1)}, u32[]{:S(2)}, u32[]{:S(2)}) collective-permute-start(f32[32,32]{0,1:T(8,128)S(1)} %bitcast.31), channel_id=1, source_target_pairs={{0,1},{1,2},{2,3},{3,0},{4,5},{5,6},{6,7},{7,4},{8,9},{9,10},{10,1... | collective-permute-start | bytes 12296 | tf_op jit(solution)/shard_map/ppermute | solution.py:42
  5.1 6.4 %collective-permute-start.1 = (f32[32,32]{0,1:T(8,128)S(1)}, f32[32,32]{0,1:T(8,128)S(1)}, u32[]{:S(2)}, u32[]{:S(2)}) collective-permute-start(f32[32,32]{0,1:T(8,128)S(1)} %bitcast.32), channel_id=1, source_target_pairs={{0,2},{1,3},{2,0},{3,1},{4,6},{5,7},{6,4},{7,5},{8,10},{9,11},{10,... | collective-permute-start | bytes 12296 | tf_op jit(solution)/shard_map/ppermute | solution.py:42
  6.6 4.8 %collective-permute-start.2 = (f32[32,32]{0,1:T(8,128)S(1)}, f32[32,32]{0,1:T(8,128)S(1)}, u32[]{:S(2)}, u32[]{:S(2)}) collective-permute-start(f32[32,32]{0,1:T(8,128)S(1)} %bitcast.33), channel_id=1, source_target_pairs={{0,3},{1,0},{2,1},{3,2},{4,7},{5,4},{6,5},{7,6},{8,11},{9,8},{10,9... | collective-permute-start | bytes 12296 | tf_op jit(solution)/shard_map/ppermute | solution.py:42
  16.0 24.0 %all-to-all-start = ((f32[64,1,512]{2,1,0:T(1,128)}), f32[64,1,512]{2,1,0:T(1,128)S(1)}, u32[]{:S(2)}, u32[]{:S(2)}) async-start(f32[64,1,512]{2,1,0:T(1,128)} %mul.245), calls=%async_computation | async-start | bytes 262144 | tf_op jit(solution)/shard_map/all_to_all | solution.py:95
  58.7 5.3 %collective-permute-start.3 = (f32[32,32]{0,1:T(8,128)S(1)}, f32[32,32]{0,1:T(8,128)S(1)}, u32[]{:S(2)}, u32[]{:S(2)}) collective-permute-start(f32[32,32]{0,1:T(8,128)S(1)} %maximum_multiply_fusion.2), channel_id=1, source_target_pairs={{0,1},{1,2},{2,3},{3,0},{4,5},{5,6},{6,7},{7,4},{8,9},{9,10},{10,1... | collective-permute-start | bytes 12296 | tf_op jit(solution)/shard_map/ppermute | solution.py:42
  63.1 3.1 %collective-permute-start.4 = (f32[32,32]{0,1:T(8,128)S(1)}, f32[32,32]{0,1:T(8,128)S(1)}, u32[]{:S(2)}, u32[]{:S(2)}) collective-permute-start(f32[32,32]{0,1:T(8,128)S(1)} %maximum_multiply_fusion.2), channel_id=1, source_target_pairs={{0,2},{1,3},{2,0},{3,1},{4,6},{5,7},{6,4},{7,5},{8,10},{9,11},{10,... | collective-permute-start | bytes 12296 | tf_op jit(solution)/shard_map/ppermute | solution.py:42
  63.9 3.2 %collective-permute-start.5 = (f32[32,32]{0,1:T(8,128)S(1)}, f32[32,32]{0,1:T(8,128)S(1)}, u32[]{:S(2)}, u32[]{:S(2)}) collective-permute-start(f32[32,32]{0,1:T(8,128)S(1)} %maximum_multiply_fusion.2), channel_id=1, source_target_pairs={{0,3},{1,0},{2,1},{3,2},{4,7},{5,4},{6,5},{7,6},{8,11},{9,8},{10,9... | collective-permute-start | bytes 12296 | tf_op jit(solution)/shard_map/ppermute | solution.py:42
